TPU v7x, 256 devices: a whole 4x4x8 slice. The times are simulated.
256 devices in a mesh: cells: 16 (over z, core), tracer: 16 (over y, x).
Axes of the slice: x: 4, y: 4, z: 8, core: 2. Of those that a mesh axis runs over, the one named last changes fastest.
Arguments:
- adjoint: float32 [64, 65536], P('tracer', 'cells'), may hold values from -6 to 6
- blocks: float32 [2048, 128, 128], P('cells'), may hold values from -0.375 to 0.375
- row_ptr: int32 [16, 33], P('cells'), may hold values from 0 to 128, as said below
- col_idx: int32 [2048], P('cells'), may hold values from 0 to 511, as said below
- regime: int32 [512], P('cells'), may hold values from 0 to 7
- jac: float32 [8, 64, 64], replicated, as said below
Outputs:
- sensitivity: float32 [64, 65536], P('tracer', 'cells')
Inputs may be any that keep to these rules, and one draw needn't show every extreme that they name: row_ptr[d, 0] = 0 and each block row holds 1 to 4 slots; some index of cells uses all 128 slots. `col_idx`: the first slot of each block row is its diagonal block; a live slot's column lies at most 32 blocks away from its block row, counted cyclically over the 512 blocks, and that distance is reached; slots past row_ptr[d, 32] hold any valid column. `jac`: each regime's matrix has diagonal entries of order one and off-diagonal couplings of order 0.1 between every pair of species.
All inputs are finite; a program needn't handle non-finite values.
Results may differ from a plain program's by a relative error of at most 0.0001.
Values sent between devices are 32-bit elements; how exact they have to be, the bound alone decides.
No kernel may reach another device: no remote copies, remote signals or barrier semaphores. Data moves between devices by JAX's collectives and lax.ppermute only.
A program may use at most 64 MiB of HBM per device.

v0:
```python
import jax
import jax.numpy as jnp
from jax import lax
from jax.sharding import PartitionSpec as P

BLOCK = 128
STEPS = 2


def with_halo(cells, sides, width):
    for axis, dim in sides:
        count = lax.axis_size(axis)
        head = lax.slice_in_dim(cells, 0, width, axis=dim)
        tail = lax.slice_in_dim(cells, cells.shape[dim] - width, cells.shape[dim], axis=dim)
        cells = jnp.concatenate(
            [
                lax.ppermute(tail, axis, [(i, (i + 1) % count) for i in range(count)]),
                cells,
                lax.ppermute(head, axis, [((i + 1) % count, i) for i in range(count)]),
            ],
            axis=dim,
        )
    return cells


def chemistry(moved, cell_regime, jac_table):
    result = jnp.zeros((jac_table.shape[2], moved.shape[1]), jnp.float32)
    for regime_id in range(jac_table.shape[0]):
        reacted = jnp.einsum(
            "ts,tc->sc", jac_table[regime_id], moved, precision=lax.Precision.HIGHEST
        )
        result = result + jnp.where(
            cell_regime[None, :] == regime_id, reacted, jnp.zeros_like(reacted)
        )
    return result


def body(adjoint, blocks, row_ptr, col_idx, regime, jac):
    spec_dev, cells_dev = adjoint.shape
    nb_dev = cells_dev // BLOCK
    cell_devices = lax.axis_size("cells")
    cell_index = lax.axis_index("cells")
    tracer_index = lax.axis_index("tracer")
    nb_total = nb_dev * cell_devices
    pointers = row_ptr[0]
    slot_count = blocks.shape[0]
    slot_ids = jnp.arange(slot_count)
    member = (
        (slot_ids[None, :] >= pointers[:-1, None]) & (slot_ids[None, :] < pointers[1:, None])
    ).astype(jnp.float32)
    live_slot = slot_ids < pointers[-1]
    local_col = jnp.mod(col_idx - (cell_index - 1) * nb_dev, nb_total)
    local_col = jnp.where(live_slot, local_col, 0)
    cell_regime = jnp.repeat(regime, BLOCK)
    adjoint_field = adjoint
    for hour_step in range(STEPS):
        extended = with_halo(adjoint_field, (("cells", 1),), cells_dev)
        extended_blocks = extended.reshape(spec_dev, 3 * nb_dev, BLOCK)
        picked = jnp.take(extended_blocks, local_col, axis=1, mode="clip")
        picked = jnp.where(live_slot[None, :, None], picked, jnp.zeros_like(picked))
        products = jnp.einsum("sij,qsj->qsi", blocks, picked, precision=lax.Precision.HIGHEST)
        moved = jnp.einsum(
            "rs,qsi->qri", member, products, precision=lax.Precision.HIGHEST
        ).reshape(spec_dev, cells_dev)
        whole = lax.all_gather(moved, "tracer", axis=0, tiled=True)
        species_rows = lax.dynamic_slice_in_dim(jac, tracer_index * spec_dev, spec_dev, 2)
        adjoint_field = chemistry(whole, cell_regime, species_rows)
    return adjoint_field


def solution(mesh):
    return jax.shard_map(
        body,
        mesh=mesh,
        in_specs=(
            P("tracer", "cells"),
            P("cells", None, None),
            P("cells", None),
            P("cells"),
            P("cells"),
            P(),
        ),
        out_specs=P("tracer", "cells"),
        check_vma=False,
    )
```

profile of v0, /device:TPU:2, one launch (start us, length us, event | category | flops | bytes accessed | tf_op | source)
XLA Modules:
  0.0 172.9 jit_solution(1758554243512436759)
XLA Ops:
  6.5 0.0 copy-start
  6.5 0.0 copy-start.1
  6.5 0.0 all-gather.5.cloned.1.call-start
  6.5 0.0 collective-permute-start
  6.6 5.3 %collective-permute-start.1 = (f32[4,4096]{1,0:T(4,128)}, f32[4,4096]{1,0:T(4,128)S(1)}, u32[]{:S(2)}, u32[]{:S(2)}) collective-permute-start(f32[4,4096]{1,0:T(4,128)} %param.6), channel_id=1, source_target_pairs={{16,0},{32,16},{48,32},{64,48},{80,64},{96,80},{112,96},{128,112},... | collective-permute-start | bytes 196616 | tf_op jit(solution)/shard_map/ppermute | solution.py:19
  11.9 1.2 slice.45
  13.1 0.8 slice_bitcast_fusion.1
  13.9 1.3 fusion.48
  15.2 0.7 iota_compare_fusion.2
  15.9 0.0 collective-permute-done
  15.9 0.0 collective-permute-done.1
  15.9 0.9 maximum_bitcast_fusion
  16.8 0.8 gather_fusion
  17.5 15.5 %convolution_bitcast_fusion.1 = f32[4,128,128]{2,0,1:T(4,128)S(1)} fusion(f32[128,128,128]{2,1,0:T(8,128)} %param.7, f32[128,4,128]{2,1,0:T(4,128)S(1)} %gather_fusion, pred[128]{0:T(512)(128)(4,1)S(1)} %iota_compare_fusion.2), kind=kOutput, calls=%fused_computation.33 | convolution fusion | flops 100728832 | bytes 8913024 | tf_op jit(solution)/shard_map/sij,qsj->qsi/dot_general | solution.py:61
  33.0 0.2 convolution_bitcast_fusion.3
  33.3 0.7 reshape.118
  33.9 0.0 all-gather.5.cloned.1.call-update
  34.0 0.0 all-gather.7.cloned.1.call-start
  34.0 0.0 copy-done.1
  34.0 0.1 broadcast_bitcast_fusion.6
  34.1 0.1 broadcast_bitcast_fusion.4
  34.2 0.1 broadcast_bitcast_fusion.2
  34.3 0.1 broadcast_bitcast_fusion
  34.4 47.5 %all-gather.5.cloned.1.call-done = f32[16,4,4096]{2,1,0:T(4,128)} async-done(((f32[1,4,4096]{2,1,0:T(4,128)}), f32[16,4,4096]{2,1,0:T(4,128)}) %all-gather.5.cloned.1.call-update) | async-done | bytes 1048592 | tf_op jit(solution)/shard_map/all_gather | solution.py:65
  81.8 1.6 reshape.119
  83.4 0.0 copy-done
  83.4 0.7 convolution_select_fusion.15
  84.1 0.7 fusion.13
  84.8 0.7 fusion.12
  85.5 0.7 fusion.11
  86.1 0.7 fusion.10
  86.8 0.7 fusion.9
  87.5 0.7 fusion.8
  88.1 0.7 fusion.7
  88.8 0.0 collective-permute-start.2
  88.8 2.9 %collective-permute-start.3 = (f32[4,4096]{1,0:T(4,128)S(1)}, f32[4,4096]{1,0:T(4,128)S(1)}, u32[]{:S(2)}, u32[]{:S(2)}) collective-permute-start(f32[4,4096]{1,0:T(4,128)S(1)} %fusion.7), channel_id=1, source_target_pairs={{16,0},{32,16},{48,32},{64,48},{80,64},{96,80},{112,96},{128,112},... | collective-permute-start | bytes 196616 | tf_op jit(solution)/shard_map/ppermute | solution.py:19
  91.8 1.9 %collective-permute-done.2 = f32[4,4096]{1,0:T(4,128)S(1)} collective-permute-done((f32[4,4096]{1,0:T(4,128)S(1)}, f32[4,4096]{1,0:T(4,128)S(1)}, u32[]{:S(2)}, u32[]{:S(2)}) %collective-permute-start.2) | collective-permute-done | bytes 65568 | tf_op jit(solution)/shard_map/ppermute | solution.py:17
  93.7 0.0 collective-permute-done.3
  93.8 0.8 gather_fusion.1
  94.5 15.7 %convolution_bitcast_fusion = f32[4,128,128]{2,0,1:T(4,128)S(1)} fusion(f32[128,128,128]{2,1,0:T(8,128)} %param.7, f32[128,4,128]{2,1,0:T(4,128)S(1)} %gather_fusion.1, pred[128]{0:T(512)(128)(4,1)S(1)} %iota_compare_fusion.2), kind=kOutput, calls=%fused_computation.32 | convolution fusion | flops 100728832 | bytes 8913024 | tf_op jit(solution)/shard_map/sij,qsj->qsi/dot_general | solution.py:61
  110.2 0.2 convolution_bitcast_fusion.2
  110.5 0.7 reshape.120
  111.1 0.0 all-gather.7.cloned.1.call-update
  111.2 47.4 %all-gather.7.cloned.1.call-done = f32[16,4,4096]{2,1,0:T(4,128)} async-done(((f32[1,4,4096]{2,1,0:T(4,128)}), f32[16,4,4096]{2,1,0:T(4,128)}) %all-gather.7.cloned.1.call-update) | async-done | bytes 1048592 | tf_op jit(solution)/shard_map/all_gather | solution.py:65
  158.5 1.6 reshape.121
  160.1 0.7 convolution_select_fusion.7
  160.8 0.7 fusion.6
  161.4 0.7 fusion.5
  162.1 0.7 fusion.4
  162.8 0.7 fusion.3
  163.5 0.7 fusion.2
  164.1 0.7 fusion.1
  164.8 1.3 fusion
  (3 shorter events, 0.1 us)
Async XLA Ops:
  6.5 76.9 %copy-start = (f32[8,64,64]{2,1,0:T(8,128)S(1)}, f32[8,64,64]{2,1,0:T(8,128)}, u32[]{:S(2)}) copy-start(f32[8,64,64]{2,1,0:T(8,128)} %param.11) | copy-start | bytes 393220
  6.5 27.5 %copy-start.1 = (s32[32]{0:T(128)S(1)}, s32[32]{0:T(128)}, u32[]{:S(2)}) copy-start(s32[32]{0:T(128)} %param.10) | copy-start | bytes 388
  6.5 75.3 %all-gather.5.cloned.1.call-start = ((), (), s32[]{:S(2)}) async-start(), calls=%async_computation | async-start | bytes 1114112 | tf_op jit(solution)/shard_map/all_gather | solution.py:65
  6.5 9.3 %collective-permute-start = (f32[4,4096]{1,0:T(4,128)}, f32[4,4096]{1,0:T(4,128)S(1)}, u32[]{:S(2)}, u32[]{:S(2)}) collective-permute-start(f32[4,4096]{1,0:T(4,128)} %param.6), channel_id=1, source_target_pairs={{0,16},{16,32},{32,48},{48,64},{64,80},{80,96},{96,112},{112,128},... | collective-permute-start | bytes 196616 | tf_op jit(solution)/shard_map/ppermute | solution.py:17
  6.6 9.3 %collective-permute-start.1 = (f32[4,4096]{1,0:T(4,128)}, f32[4,4096]{1,0:T(4,128)S(1)}, u32[]{:S(2)}, u32[]{:S(2)}) collective-permute-start(f32[4,4096]{1,0:T(4,128)} %param.6), channel_id=1, source_target_pairs={{16,0},{32,16},{48,32},{64,48},{80,64},{96,80},{112,96},{128,112},... | collective-permute-start | bytes 196616 | tf_op jit(solution)/shard_map/ppermute | solution.py:19
  34.0 124.5 %all-gather.7.cloned.1.call-start = ((), (), s32[]{:S(2)}) async-start(), calls=%async_computation.1 | async-start | bytes 1114112 | tf_op jit(solution)/shard_map/all_gather | solution.py:65
  88.8 4.9 %collective-permute-start.2 = (f32[4,4096]{1,0:T(4,128)S(1)}, f32[4,4096]{1,0:T(4,128)S(1)}, u32[]{:S(2)}, u32[]{:S(2)}) collective-permute-start(f32[4,4096]{1,0:T(4,128)S(1)} %fusion.7), channel_id=1, source_target_pairs={{0,16},{16,32},{32,48},{48,64},{64,80},{80,96},{96,112},{112,128},... | collective-permute-start | bytes 196616 | tf_op jit(solution)/shard_map/ppermute | solution.py:17
  88.8 4.9 %collective-permute-start.3 = (f32[4,4096]{1,0:T(4,128)S(1)}, f32[4,4096]{1,0:T(4,128)S(1)}, u32[]{:S(2)}, u32[]{:S(2)}) collective-permute-start(f32[4,4096]{1,0:T(4,128)S(1)} %fusion.7), channel_id=1, source_target_pairs={{16,0},{32,16},{48,32},{64,48},{80,64},{96,80},{112,96},{128,112},... | collective-permute-start | bytes 196616 | tf_op jit(solution)/shard_map/ppermute | solution.py:19
Sparse Core Ops, SparseCore 0:
  34.1 47.7 all-gather.4
  111.3 47.1 all-gather.6
where the time goes:
time: 173 us
  waiting for transfers between devices  96.8 us (56%)
  matrix products  42.9 us (25%)
  between operations  13.6 us (8%)
  local copies, waits for them, and re-layouts  8.35 us (5%)
  starting transfers between devices  8.32 us (5%)
  other arithmetic  2.91 us (2%)
    all_gather x2, waiting for transfers between devices, body(): whole = lax.all_gather(moved, 'tracer', axis=0, tiled=True)  94.8 us
    dot_general x2, matrix products, body(): jnp.einsum('sij,qsj->qsi', blocks, picked, precision=lax.Precision.HIGHEST)  31.2 us
    dot_general x16, matrix products, chemistry(): jnp.einsum('ts,tc->sc', jac_table[regime_id], moved, precision=lax.Precis...  11.3 us
    ppermute x2, starting transfers between devices, with_halo(): lax.ppermute(head, axis, [((i + 1) % count, i) for i in range(count)])  8.25 us
    unnamed x8, local copies, waits for them, and re-layouts  4.5 us
  transfers between devices with their start and end apart: 6, of which 3 were waited for; matrix products, arithmetic and copies ran while one was open for 2% of the time, Pallas kernels for 0%

commit v1 on v0

--- a/solution.py
+++ b/solution.py
@@ -62,7 +62,15 @@
         moved = jnp.einsum(
             "rs,qsi->qri", member, products, precision=lax.Precision.HIGHEST
         ).reshape(spec_dev, cells_dev)
-        whole = lax.all_gather(moved, "tracer", axis=0, tiled=True)
+        whole = jnp.concatenate(
+            lax.all_to_all(
+                jnp.stack([moved] * lax.psum(1, axis_name="tracer")),
+                axis_name="tracer",
+                split_axis=0,
+                concat_axis=0,
+            ),
+            axis=0,
+        )
         species_rows = lax.dynamic_slice_in_dim(jac, tracer_index * spec_dev, spec_dev, 2)
         adjoint_field = chemistry(whole, cell_regime, species_rows)
     return adjoint_field

time: 173 us -> 105 us (0.61)
  waiting for transfers between devices: 96.8 us -> 15 us
  blocking collectives: 0 us -> 20.9 us
  between operations: 13.6 us -> 0.23 us
  starting transfers between devices: 8.32 us -> 15.8 us
  local copies, waits for them, and re-layouts: 8.35 us -> 6.04 us
    all_gather x2 -> x0, waiting for transfers between devices: 94.8 us -> none  [body(): whole = lax.all_gather(moved, 'tracer', axis=0, tiled=True)]
    all_to_all x0 -> x1, blocking collectives: none -> 20.9 us  [body(): lax.all_to_all(jnp.stack([moved] * lax.psum(1, axis_name='tracer')), axis...]
    all_to_all x0 -> x1, waiting for transfers between devices: none -> 13.1 us  [body(): lax.all_to_all(jnp.stack([moved] * lax.psum(1, axis_name='tracer')), axis...]
    all_to_all x0 -> x1, starting transfers between devices: none -> 7.48 us  [body(): lax.all_to_all(jnp.stack([moved] * lax.psum(1, axis_name='tracer')), axis...]
    unnamed x8 -> x6, local copies, waits for them, and re-layouts: 4.5 us -> 0.1 us
  transfers between devices with their start and end apart: 6 -> 5, of which waited for: 3 -> 2; matrix products, arithmetic and copies ran while one was open for 2% -> 4% of each run, Pallas kernels for 0% -> 0%
where the time goes in v1:
time: 105 us; the launch traced here: 104 us
  matrix products  42.8 us (41%)
  blocking collectives  20.9 us (20%)
  starting transfers between devices  15.8 us (15%)
  waiting for transfers between devices  15 us (14%)
  local copies, waits for them, and re-layouts  6.04 us (6%)
  other arithmetic  2.91 us (3%)
    dot_general x2, matrix products, body(): jnp.einsum('sij,qsj->qsi', blocks, picked, precision=lax.Precision.HIGHEST)  31 us
    all_to_all x1, blocking collectives, body(): lax.all_to_all(jnp.stack([moved] * lax.psum(1, axis_name='tracer')), axis...  20.9 us
    all_to_all x1, waiting for transfers between devices, body(): lax.all_to_all(jnp.stack([moved] * lax.psum(1, axis_name='tracer')), axis...  13.1 us
    dot_general x16, matrix products, chemistry(): jnp.einsum('ts,tc->sc', jac_table[regime_id], moved, precision=lax.Precis...  11.3 us
    ppermute x2, starting transfers between devices, with_halo(): lax.ppermute(head, axis, [((i + 1) % count, i) for i in range(count)])  8.25 us
    all_to_all x1, starting transfers between devices, body(): lax.all_to_all(jnp.stack([moved] * lax.psum(1, axis_name='tracer')), axis...  7.48 us
  transfers between devices with their start and end apart: 5, of which 2 were waited for; matrix products, arithmetic and copies ran while one was open for 4% of the time, Pallas kernels for 0%

profile of v1, /device:TPU:2, one launch (start us, length us, event | category | flops | bytes accessed | tf_op | source)
XLA Modules:
  0.0 103.6 jit_solution(2038492601452350623)
XLA Ops:
  0.0 0.0 copy-start
  0.0 0.0 copy-start.1
  0.0 0.0 collective-permute-start
  0.0 5.3 %collective-permute-start.1 = (f32[4,4096]{1,0:T(4,128)}, f32[4,4096]{1,0:T(4,128)S(1)}, u32[]{:S(2)}, u32[]{:S(2)}) collective-permute-start(f32[4,4096]{1,0:T(4,128)} %param.6), channel_id=1, source_target_pairs={{16,0},{32,16},{48,32},{64,48},{80,64},{96,80},{112,96},{128,112},... | collective-permute-start | bytes 196616 | tf_op jit(solution)/shard_map/ppermute | solution.py:19
  5.3 1.2 %slice.45 = s32[1,1]{1,0:T(1,128)} slice(s32[1,33]{1,0:T(1,128)} %param.8), slice={[0:1], [32:33]} | slice | bytes 8 | tf_op jit(solution)/shard_map/slice | solution.py:51
  6.6 0.8 slice_bitcast_fusion.1
  7.4 1.3 %fusion.52 = s32[128]{0:T(128)S(1)} fusion(s32[128]{0:T(128)} %param.9, s32[]{:T(128)S(6)} %mul.8, s32[]{:T(128)} %bitcast.2), kind=kLoop, calls=%fused_computation.96 | loop fusion | flops 1792 | bytes 1032 | tf_op jit(solution)/shard_map/jit(_where)/select_n | solution.py:53
  8.7 0.7 iota_compare_fusion.2
  9.3 0.0 collective-permute-done
  9.3 0.0 collective-permute-done.1
  9.4 0.9 maximum_bitcast_fusion
  10.2 0.8 gather_fusion
  11.0 15.5 %fusion.18 = f32[128,4,128]{2,1,0:T(4,128)S(1)} fusion(f32[128,128,128]{2,1,0:T(8,128)} %param.7, f32[128,4,128]{2,1,0:T(4,128)S(1)} %gather_fusion, pred[128]{0:T(512)(128)(4,1)S(1)} %iota_compare_fusion.2), kind=kOutput, calls=%fused_computation.38 | convolution fusion | flops 100728832 | bytes 8913024 | tf_op jit(solution)/shard_map/sij,qsj->qsi/dot_general | solution.py:61
  26.5 0.2 convolution_bitcast_fusion.1
  26.8 1.2 %stack.6 = f32[16,4,4096]{2,1,0:T(4,128)} broadcast(f32[4,4096]{1,0:T(4,128)S(1)} %bitcast.103), dimensions={1,2} | broadcast | bytes 1114112 | tf_op jit(solution)/shard_map/stack | solution.py:67
  28.0 7.5 %all-to-all-start = ((f32[16,4,4096]{2,1,0:T(4,128)}), f32[16,4,4096]{2,1,0:T(4,128)S(1)}, u32[]{:S(2)}, u32[]{:S(2)}) async-start(f32[16,4,4096]{2,1,0:T(4,128)} %stack.6), calls=%async_computation | async-start | bytes 2097152 | tf_op jit(solution)/shard_map/all_to_all | solution.py:66
  35.5 0.0 copy-done.1
  35.5 0.1 broadcast_bitcast_fusion.6
  35.6 0.1 broadcast_bitcast_fusion.4
  35.6 0.1 broadcast_bitcast_fusion.2
  35.7 0.1 broadcast_bitcast_fusion
  35.8 13.1 %all-to-all-done = f32[16,4,4096]{2,1,0:T(4,128)S(1)} async-done(((f32[16,4,4096]{2,1,0:T(4,128)}), f32[16,4,4096]{2,1,0:T(4,128)S(1)}, u32[]{:S(2)}, u32[]{:S(2)}) %all-to-all-start) | async-done | bytes 1048608 | tf_op jit(solution)/shard_map/all_to_all | solution.py:66
  48.9 0.4 reshape.101
  49.2 0.0 copy-done
  49.2 0.7 convolution_select_fusion.15
  49.9 0.7 fusion.13
  50.6 0.7 fusion.12
  51.3 0.7 fusion.11
  51.9 0.7 fusion.10
  52.6 0.7 fusion.9
  53.3 0.7 fusion.8
  54.0 0.7 fusion.7
  54.6 0.0 collective-permute-start.2
  54.6 2.9 %collective-permute-start.3 = (f32[4,4096]{1,0:T(4,128)S(1)}, f32[4,4096]{1,0:T(4,128)S(1)}, u32[]{:S(2)}, u32[]{:S(2)}) collective-permute-start(f32[4,4096]{1,0:T(4,128)S(1)} %fusion.7), channel_id=1, source_target_pairs={{16,0},{32,16},{48,32},{64,48},{80,64},{96,80},{112,96},{128,112},... | collective-permute-start | bytes 196616 | tf_op jit(solution)/shard_map/ppermute | solution.py:19
  57.6 1.9 %collective-permute-done.2 = f32[4,4096]{1,0:T(4,128)S(1)} collective-permute-done((f32[4,4096]{1,0:T(4,128)S(1)}, f32[4,4096]{1,0:T(4,128)S(1)}, u32[]{:S(2)}, u32[]{:S(2)}) %collective-permute-start.2) | collective-permute-done | bytes 65568 | tf_op jit(solution)/shard_map/ppermute | solution.py:17
  59.5 0.0 collective-permute-done.3
  59.6 0.8 gather_fusion.1
  60.3 15.5 %fusion.15 = f32[128,4,128]{2,1,0:T(4,128)S(1)} fusion(f32[128,128,128]{2,1,0:T(8,128)} %param.7, f32[128,4,128]{2,1,0:T(4,128)S(1)} %gather_fusion.1, pred[128]{0:T(512)(128)(4,1)S(1)} %iota_compare_fusion.2), kind=kOutput, calls=%fused_computation.35 | convolution fusion | flops 100728832 | bytes 8913024 | tf_op jit(solution)/shard_map/sij,qsj->qsi/dot_general | solution.py:61
  75.8 0.2 convolution_bitcast_fusion
  76.1 0.2 stack.7
  76.3 20.9 %all_to_all.10 = f32[16,4,4096]{2,1,0:T(4,128)S(1)} all-to-all(f32[16,4,4096]{2,1,0:T(4,128)S(1)} %stack.7), channel_id=1, replica_groups=mesh['cells'=16,'tracer'=16] {'tracer'}, dimensions={0} | all-to-all | bytes 2097152 | tf_op jit(solution)/shard_map/all_to_all | solution.py:66
  97.2 0.4 reshape.103
  97.6 0.7 convolution_select_fusion.7
  98.3 0.7 fusion.6
  98.9 0.7 fusion.5
  99.6 0.7 fusion.4
  100.3 0.7 fusion.3
  100.9 0.7 fusion.2
  101.6 0.7 fusion.1
  102.3 1.3 %fusion = f32[4,4096]{1,0:T(4,128)} fusion(f32[4,4096]{1,0:T(4,128)S(1)} %fusion.1, f32[64,4096]{1,0:T(8,128)S(1)} %reshape.103, pred[4096]{0:T(1024)(128)(4,1)S(1)} %get-tuple-element.15, f32[8,64,64]{2,1,0:T(8,128)S(1)} %copy-done, s32[]{:T(128)S(6)} %add.75, s32[]{:T(128)S(6)} %select_n.71), kind=kOutput, calls=%fused_computation.3 | convolution fusion | flops 12615680 | bytes 1216520 | tf_op jit(solution)/shard_map/ts,tc->sc/dot_general | solution.py:29
  (5 shorter events, 0.2 us)
Async XLA Ops:
  0.0 49.2 %copy-start = (f32[8,64,64]{2,1,0:T(8,128)S(1)}, f32[8,64,64]{2,1,0:T(8,128)}, u32[]{:S(2)}) copy-start(f32[8,64,64]{2,1,0:T(8,128)} %param.11) | copy-start | bytes 393220
  0.0 35.5 %copy-start.1 = (s32[32]{0:T(128)S(1)}, s32[32]{0:T(128)}, u32[]{:S(2)}) copy-start(s32[32]{0:T(128)} %param.10) | copy-start | bytes 388
  0.0 9.3 %collective-permute-start = (f32[4,4096]{1,0:T(4,128)}, f32[4,4096]{1,0:T(4,128)S(1)}, u32[]{:S(2)}, u32[]{:S(2)}) collective-permute-start(f32[4,4096]{1,0:T(4,128)} %param.6), channel_id=1, source_target_pairs={{0,16},{16,32},{32,48},{48,64},{64,80},{80,96},{96,112},{112,128},... | collective-permute-start | bytes 196616 | tf_op jit(solution)/shard_map/ppermute | solution.py:17
  0.0 9.3 %collective-permute-start.1 = (f32[4,4096]{1,0:T(4,128)}, f32[4,4096]{1,0:T(4,128)S(1)}, u32[]{:S(2)}, u32[]{:S(2)}) collective-permute-start(f32[4,4096]{1,0:T(4,128)} %param.6), channel_id=1, source_target_pairs={{16,0},{32,16},{48,32},{64,48},{80,64},{96,80},{112,96},{128,112},... | collective-permute-start | bytes 196616 | tf_op jit(solution)/shard_map/ppermute | solution.py:19
  28.0 20.9 %all-to-all-start = ((f32[16,4,4096]{2,1,0:T(4,128)}), f32[16,4,4096]{2,1,0:T(4,128)S(1)}, u32[]{:S(2)}, u32[]{:S(2)}) async-start(f32[16,4,4096]{2,1,0:T(4,128)} %stack.6), calls=%async_computation | async-start | bytes 2097152 | tf_op jit(solution)/shard_map/all_to_all | solution.py:66
  54.6 4.9 %collective-permute-start.2 = (f32[4,4096]{1,0:T(4,128)S(1)}, f32[4,4096]{1,0:T(4,128)S(1)}, u32[]{:S(2)}, u32[]{:S(2)}) collective-permute-start(f32[4,4096]{1,0:T(4,128)S(1)} %fusion.7), channel_id=1, source_target_pairs={{0,16},{16,32},{32,48},{48,64},{64,80},{80,96},{96,112},{112,128},... | collective-permute-start | bytes 196616 | tf_op jit(solution)/shard_map/ppermute | solution.py:17
  54.6 4.9 %collective-permute-start.3 = (f32[4,4096]{1,0:T(4,128)S(1)}, f32[4,4096]{1,0:T(4,128)S(1)}, u32[]{:S(2)}, u32[]{:S(2)}) collective-permute-start(f32[4,4096]{1,0:T(4,128)S(1)} %fusion.7), channel_id=1, source_target_pairs={{16,0},{32,16},{48,32},{64,48},{80,64},{96,80},{112,96},{128,112},... | collective-permute-start | bytes 196616 | tf_op jit(solution)/shard_map/ppermute | solution.py:19
